TPU v7x, 32 devices: a whole 2x2x4 slice. The times are simulated.
32 devices in a mesh: grp: 4 (over z), band: 8 (over y, x, core).
Axes of the slice: x: 2, y: 2, z: 4, core: 2. Of those that a mesh axis runs over, the one named last changes fastest.
Arguments:
- orbitals: float32 [18432, 512], P('grp', 'band'), may hold values from -6 to 6
- requests: int32 [32, 6], replicated, may hold values from -1 to 11, as said below
- coulomb: float32 [96, 1536, 1536], P(('grp', 'band')), may hold values from -0.001953125 to 0.001953125
Outputs:
- exchange_rows: float32 [18432, 512], P('grp', 'band')
Inputs may be any that keep to these rules, and one draw needn't show every extreme that they name: `requests`: entries 2q and 2q + 1 of row d are the two blocks of slot q of device d, the first not above the second, or both -1 for an empty slot; every pair of the 12 blocks, a block with itself included, stands in exactly one slot.
All inputs are finite; a program needn't handle non-finite values.
Results may differ from a plain program's by a relative error of at most 0.0003.
Values sent between devices are 32-bit elements; how exact they have to be, the bound alone decides.
No kernel may reach another device: no remote copies, remote signals or barrier semaphores. Data moves between devices by JAX's collectives and lax.ppermute only.
A program may use at most 256 MiB of HBM per device.

v0:
```python
import jax
import jax.numpy as jnp
from jax import lax
from jax.sharding import PartitionSpec as P

PRECISION = lax.Precision.HIGH


def band_exchange(outgoing):
    return lax.all_to_all(outgoing, "band", split_axis=0, concat_axis=0, tiled=True)


def line_gather(x, axis, count, riders=()):
    index = lax.axis_index(axis)
    spare = jnp.zeros((count + 1,) + x.shape, x.dtype)
    spare = lax.dynamic_update_index_in_dim(spare, x, index, 0)
    rightward, leftward = (x, x)
    carried = []
    for step in range(1, count):
        rider = step - 1 < len(riders)
        if rider:
            rightward, leftward, load = lax.optimization_barrier(
                (rightward, leftward, riders[step - 1])
            )
        rightward = lax.ppermute(rightward, axis, [(i, i + 1) for i in range(step - 1, count - 1)])
        leftward = lax.ppermute(leftward, axis, [(i + 1, i) for i in range(0, count - step)])
        if rider:
            rightward, leftward, load = lax.optimization_barrier(
                (rightward, leftward, band_exchange(load))
            )
            carried.append(load)
        from_left = jnp.where(index >= step, index - step, count)
        from_right = jnp.where(index + step < count, index + step, count)
        spare = lax.dynamic_update_index_in_dim(spare, rightward, from_left, 0)
        spare = lax.dynamic_update_index_in_dim(spare, leftward, from_right, 0)
    carried += [band_exchange(load) for load in riders[len(carried) :]]
    return (spare[:count], carried)


def line_reduce(parts, axis, count, riders=()):
    index = lax.axis_index(axis)

    def part_for(target):
        return lax.dynamic_index_in_dim(parts, jnp.clip(target, 0, count - 1), 0, keepdims=False)

    rightward = jnp.zeros(parts.shape[1:], parts.dtype)
    leftward = jnp.zeros(parts.shape[1:], parts.dtype)
    carried = []
    for step in range(1, count):
        send_right = rightward + part_for(index + count - step)
        send_left = leftward + part_for(index - count + step)
        rider = step - 1 < len(riders)
        if rider:
            send_right, send_left, load = lax.optimization_barrier(
                (send_right, send_left, riders[step - 1])
            )
        rightward = lax.ppermute(send_right, axis, [(i, i + 1) for i in range(0, step)])
        leftward = lax.ppermute(send_left, axis, [(i, i - 1) for i in range(count - step, count)])
        if rider:
            rightward, leftward, load = lax.optimization_barrier(
                (rightward, leftward, band_exchange(load))
            )
            carried.append(load)
    carried += [band_exchange(load) for load in riders[len(carried) :]]
    return (part_for(index) + rightward + leftward, carried)


def body(orbitals, requests, coulomb):
    group_count = lax.axis_size("grp")
    band_count = lax.axis_size("band")
    devices = group_count * band_count
    blk = coulomb.shape[1]
    orbital_width = orbitals.shape[1] * band_count
    half = orbital_width // 2
    piece_rows = blk // devices
    slot_count = coulomb.shape[0]
    block_count = orbitals.shape[0] // (band_count * piece_rows)
    col_half = orbitals.shape[1] // 2
    own_rows = [
        lax.all_to_all(
            orbitals[:, h * col_half : (h + 1) * col_half],
            "band",
            split_axis=0,
            concat_axis=1,
            tiled=True,
        )
        for h in range(2)
    ]
    group_index = lax.axis_index("grp")
    band_index = lax.axis_index("band")
    group_requests = lax.dynamic_slice_in_dim(requests, group_index * band_count, band_count, 0)
    own_pairs = lax.dynamic_index_in_dim(group_requests, band_index, 0, keepdims=False)
    one_hot = (
        group_requests[:, :, None] == jnp.arange(block_count, dtype=jnp.int32)[None, None, :]
    ).astype(jnp.float32)

    def requested(pieces, slot):
        wanted = group_requests[:, 2 * slot : 2 * slot + 2]
        wanted = jnp.where(wanted >= 0, wanted, block_count)
        outgoing = jnp.take(pieces, wanted, axis=1, mode="fill", fill_value=0.0)
        return outgoing.transpose(1, 2, 0, 3, 4)

    def shape_pieces(gathered):
        return gathered.reshape(group_count, block_count, piece_rows, half)

    first_pieces = shape_pieces(line_gather(own_rows[0], "grp", group_count)[0])
    first_loads = [requested(first_pieces, slot) for slot in range(slot_count)]
    second_pieces, first_arrived = line_gather(own_rows[1], "grp", group_count, first_loads)
    second_pieces = shape_pieces(second_pieces)
    second_arrived = [band_exchange(requested(second_pieces, slot)) for slot in range(slot_count)]
    returned = [[], []]
    held = []
    for slot in range(slot_count):
        rows = [
            arrived.transpose(1, 2, 0, 3, 4).reshape(2, blk, half)
            for arrived in (first_arrived[slot], second_arrived[slot])
        ]
        density = sum(
            (
                jnp.dot(r[0], r[1].T, precision=PRECISION, preferred_element_type=jnp.float32)
                for r in rows
            )
        )
        scale = jnp.where(own_pairs[2 * slot] == own_pairs[2 * slot + 1], 0.5, 1.0)
        kernel = density * (coulomb[slot] * scale)
        for h in range(2):
            onto_first = jnp.dot(
                kernel, rows[h][1], precision=PRECISION, preferred_element_type=jnp.float32
            )
            onto_second = jnp.dot(
                kernel.T, rows[h][0], precision=PRECISION, preferred_element_type=jnp.float32
            )
            outbound = jnp.stack([onto_first, onto_second], 0).reshape(
                2, group_count, band_count, piece_rows, half
            )
            outbound = outbound.transpose(2, 0, 1, 3, 4)
            if h == 0:
                returned[0].append(band_exchange(outbound))
            else:
                held.append(outbound)

    def sum_blocks(returned):
        gathered = jnp.concatenate(returned, axis=1)
        return jnp.einsum("srk,srgpn->gkpn", one_hot, gathered, precision=PRECISION)

    first_home, second_returned = line_reduce(sum_blocks(returned[0]), "grp", group_count, held)
    second_home, _ = line_reduce(sum_blocks(second_returned), "grp", group_count)
    home = [
        lax.all_to_all(
            rows.reshape(block_count * piece_rows, half),
            "band",
            split_axis=1,
            concat_axis=0,
            tiled=True,
        )
        for rows in (first_home, second_home)
    ]
    return jnp.concatenate(home, axis=1)


def solution(mesh):
    placed = (P("grp", "band"), P(), P(("grp", "band"), None, None))
    return jax.shard_map(
        body, mesh=mesh, in_specs=placed, out_specs=P("grp", "band"), check_vma=False
    )
```

profile of v0, /device:TPU:0, one launch (start us, length us, event | category | flops | bytes accessed | tf_op | source)
XLA Modules:
  0.0 702.9 jit_solution(11223756371621740991)
XLA Ops:
  1.7 16.1 %all_to_all.136 = f32[8,576,32]{1,2,0:T(8,128)S(1)} all-to-all(f32[8,576,32]{1,2,0:T(8,128)S(1)} %copy.177), channel_id=1, replica_groups=mesh['grp'=4,'band'=8] {'band'}, dimensions={0} | all-to-all | bytes 1179648 | tf_op jit(solution)/shard_map/all_to_all | solution.py:80
  29.3 5.8 collective-permute-done
  44.5 11.7 %collective-permute-done.3 = f32[576,256]{1,0:T(8,128)S(1)} collective-permute-done((f32[576,256]{1,0:T(8,128)}, f32[576,256]{1,0:T(8,128)S(1)}, u32[]{:S(2)}, u32[]{:S(2)}) %collective-permute-start.3) | collective-permute-done | bytes 589856 | tf_op jit(solution)/shard_map/ppermute | solution.py:26
  57.6 13.5 %collective-permute-done.5 = f32[576,256]{1,0:T(8,128)S(1)} collective-permute-done((f32[576,256]{1,0:T(8,128)S(1)}, f32[576,256]{1,0:T(8,128)S(1)}, u32[]{:S(2)}, u32[]{:S(2)}) %collective-permute-start.5) | collective-permute-done | bytes 589856 | tf_op jit(solution)/shard_map/ppermute | solution.py:26
  103.3 16.8 %all-to-all-done.2 = f32[8,2,4,48,256]{4,3,2,1,0:T(8,128)} async-done(((f32[8,2,4,48,256]{4,3,2,1,0:T(8,128)}), f32[8,2,4,48,256]{4,3,2,1,0:T(8,128)}, u32[]{:S(2)}, u32[]{:S(2)}) %all-to-all-start.2) | async-done | bytes 3145760 | tf_op jit(solution)/shard_map/all_to_all | solution.py:10
  136.4 7.2 %collective-permute-done.9 = f32[576,256]{1,0:T(8,128)} collective-permute-done((f32[576,256]{1,0:T(8,128)S(1)}, f32[576,256]{1,0:T(8,128)}, u32[]{:S(2)}, u32[]{:S(2)}) %collective-permute-start.9) | collective-permute-done | bytes 589856 | tf_op jit(solution)/shard_map/ppermute | solution.py:26
  143.7 18.8 %all-to-all-done.3 = f32[8,2,4,48,256]{4,3,2,1,0:T(8,128)} async-done(((f32[8,2,4,48,256]{4,3,2,1,0:T(8,128)}), f32[8,2,4,48,256]{4,3,2,1,0:T(8,128)}, u32[]{:S(2)}, u32[]{:S(2)}) %all-to-all-start.3) | async-done | bytes 3145760 | tf_op jit(solution)/shard_map/all_to_all | solution.py:10
  176.3 11.8 %collective-permute-done.11 = f32[576,256]{1,0:T(8,128)} collective-permute-done((f32[576,256]{1,0:T(8,128)}, f32[576,256]{1,0:T(8,128)}, u32[]{:S(2)}, u32[]{:S(2)}) %collective-permute-start.11) | collective-permute-done | bytes 589856 | tf_op jit(solution)/shard_map/ppermute | solution.py:26
  188.1 15.8 %all-to-all-done.4 = f32[8,2,4,48,256]{4,3,2,1,0:T(8,128)S(1)} async-done(((f32[8,2,4,48,256]{4,3,2,1,0:T(8,128)}), f32[8,2,4,48,256]{4,3,2,1,0:T(8,128)S(1)}, u32[]{:S(2)}, u32[]{:S(2)}) %all-to-all-start.4) | async-done | bytes 3145760 | tf_op jit(solution)/shard_map/all_to_all | solution.py:10
  231.8 26.9 %all-to-all-done.9 = f32[8,2,4,48,256]{4,3,2,1,0:T(8,128)} async-done(((f32[8,2,4,48,256]{4,3,2,1,0:T(8,128)}), f32[8,2,4,48,256]{4,3,2,1,0:T(8,128)}, u32[]{:S(2)}, u32[]{:S(2)}) %all-to-all-start.9) | async-done | bytes 3145760 | tf_op jit(solution)/shard_map/all_to_all | solution.py:10
  258.7 4.7 all-to-all-start.7
  265.8 6.5 fusion.44
  276.2 6.4 fusion.45
  291.1 6.4 fusion.46
  301.2 4.9 all-to-all-start.5
  311.9 9.6 %fusion = f32[1536,1536]{1,0:T(8,128)} fusion(f32[1536,1536]{1,0:T(8,128)S(1)} %copy-done.5, f32[1536,256]{1,0:T(8,128)S(1)} %bitcast.341, f32[1536,256]{1,0:T(8,128)S(1)} %bitcast.343, f32[3,1536,1536]{2,1,0:T(8,128)} %param.7, f32[]{:T(128)} %bitcast.81), kind=kOutput, calls=%fused_computation.7 | convolution fusion | flops 3630956544 | bytes 31457284 | tf_op jit(solution)/shard_map/dot_general | solution.py:120
  321.5 9.6 %copy.211 = f32[1536,1536]{1,0:T(8,128)} copy(f32[1536,1536]{0,1:T(8,128)} %bitcast.310) | data formatting | bytes 18874368 | tf_op jit(solution)/shard_map/dot_general | solution.py:130
  331.1 7.0 convolution_bitcast_fusion.7
  344.4 4.6 all-to-all-start.10
  351.5 12.1 %fusion.2 = f32[1536,1536]{1,0:T(8,128)} fusion(f32[1536,1536]{1,0:T(8,128)} %fusion.44, f32[1536,256]{1,0:T(8,128)S(1)} %bitcast.351, f32[1536,256]{1,0:T(8,128)S(1)} %bitcast.349, f32[3,1536,1536]{2,1,0:T(8,128)} %param.7, f32[]{:T(128)} %bitcast.39), kind=kOutput, calls=%fused_computation.11 | convolution fusion | flops 3630956544 | bytes 31457284 | tf_op jit(solution)/shard_map/dot_general | solution.py:120
  363.6 9.7 %copy.195 = f32[1536,1536]{1,0:T(8,128)} copy(f32[1536,1536]{0,1:T(8,128)} %bitcast.316) | data formatting | bytes 18874368 | tf_op jit(solution)/shard_map/dot_general | solution.py:130
  373.3 7.0 convolution_bitcast_fusion.11
  386.9 4.7 all-to-all-start.6
  394.0 11.5 %fusion.1 = f32[1536,1536]{1,0:T(8,128)} fusion(f32[1536,1536]{1,0:T(8,128)} %fusion.45, f32[1536,256]{1,0:T(8,128)S(1)} %bitcast.345, f32[1536,256]{1,0:T(8,128)S(1)} %bitcast.347, f32[3,1536,1536]{2,1,0:T(8,128)} %param.7, f32[]{:T(128)} %bitcast.60), kind=kOutput, calls=%fused_computation.9 | convolution fusion | flops 3630956544 | bytes 31457284 | tf_op jit(solution)/shard_map/dot_general | solution.py:120
  405.4 9.6 %copy.203 = f32[1536,1536]{1,0:T(8,128)} copy(f32[1536,1536]{0,1:T(8,128)} %bitcast.313) | data formatting | bytes 18874368 | tf_op jit(solution)/shard_map/dot_general | solution.py:130
  415.0 7.4 %convolution_bitcast_fusion.9 = f32[1,4,8,48,256]{4,3,2,1,0:T(8,128)S(1)} fusion(f32[4,8,48,1536]{3,2,1,0:T(8,128)} %bitcast.314, f32[1536,256,1,1]{1,0,3,2:T(8,128)} %bitcast.354), kind=kOutput, calls=%fused_computation.47 | convolution fusion | flops 3623878656 | bytes 12582912 | tf_op jit(solution)/shard_map/dot_general | solution.py:127
  434.0 7.4 %convolution_bitcast_fusion.5 = f32[1,4,8,48,256]{4,3,2,1,0:T(8,128)S(1)} fusion(f32[4,8,48,1536]{3,2,1,0:T(8,128)} %bitcast.318, f32[1536,256,1,1]{1,0,3,2:T(8,128)} %bitcast.350), kind=kOutput, calls=%fused_computation.43 | convolution fusion | flops 3623878656 | bytes 12582912 | tf_op jit(solution)/shard_map/dot_general | solution.py:127
  441.4 7.3 %convolution_bitcast_fusion.4 = f32[1,4,8,48,256]{4,3,2,1,0:T(8,128)S(1)} fusion(f32[4,8,48,1536]{3,2,1,0:T(8,128)} %bitcast.327, f32[1536,256,1,1]{1,0,3,2:T(8,128)S(1)} %bitcast.352), kind=kOutput, calls=%fused_computation.42 | convolution fusion | flops 3623878656 | bytes 12582912 | tf_op jit(solution)/shard_map/dot_general | solution.py:130
  450.8 5.3 copy.215
  456.1 5.4 copy.213
  461.5 10.4 %all-to-all-done.8 = f32[8,2,4,48,256]{4,3,2,1,0:T(8,128)} async-done(((f32[8,2,4,48,256]{4,3,2,1,0:T(8,128)}), f32[8,2,4,48,256]{4,3,2,1,0:T(8,128)}, u32[]{:S(2)}, u32[]{:S(2)}) %all-to-all-start.8) | async-done | bytes 3145760 | tf_op jit(solution)/shard_map/all_to_all | solution.py:10
  488.2 7.5 %convolution_bitcast_fusion.3 = f32[1,4,8,48,256]{4,3,2,1,0:T(8,128)S(1)} fusion(f32[4,8,48,1536]{3,2,1,0:T(8,128)} %bitcast.315, f32[1536,256,1,1]{1,0,3,2:T(8,128)} %bitcast.348), kind=kOutput, calls=%fused_computation.41 | convolution fusion | flops 3623878656 | bytes 12582912 | tf_op jit(solution)/shard_map/dot_general | solution.py:127
  506.5 6.0 collective-permute-done.12
  512.5 13.5 %all-to-all-done.11 = f32[8,2,4,48,256]{4,3,2,1,0:T(8,128)} async-done(((f32[8,2,4,48,256]{4,3,2,1,0:T(8,128)}), f32[8,2,4,48,256]{4,3,2,1,0:T(8,128)}, u32[]{:S(2)}, u32[]{:S(2)}) %all-to-all-start.11) | async-done | bytes 3145760 | tf_op jit(solution)/shard_map/all_to_all | solution.py:10
  531.4 4.7 all-to-all-start.12
  536.2 7.0 convolution_bitcast_fusion.1
  553.7 6.4 collective-permute-done.14
  560.1 13.9 %all-to-all-done.12 = f32[8,2,4,48,256]{4,3,2,1,0:T(8,128)} async-done(((f32[8,2,4,48,256]{4,3,2,1,0:T(8,128)}), f32[8,2,4,48,256]{4,3,2,1,0:T(8,128)}, u32[]{:S(2)}, u32[]{:S(2)}) %all-to-all-start.12) | async-done | bytes 3145760 | tf_op jit(solution)/shard_map/all_to_all | solution.py:10
  587.3 5.6 collective-permute-start.16
  592.9 5.4 copy.232
  598.3 5.4 copy.233
  604.8 16.1 %all-to-all-done.13 = f32[8,2,4,48,256]{4,3,2,1,0:T(8,128)S(1)} async-done(((f32[8,2,4,48,256]{4,3,2,1,0:T(8,128)}), f32[8,2,4,48,256]{4,3,2,1,0:T(8,128)S(1)}, u32[]{:S(2)}, u32[]{:S(2)}) %all-to-all-start.13) | async-done | bytes 3145760 | tf_op jit(solution)/shard_map/all_to_all | solution.py:10
  629.5 8.7 %collective-permute-done.18 = f32[12,48,256]{2,1,0:T(8,128)S(1)} collective-permute-done((f32[12,48,256]{2,1,0:T(8,128)S(1)}, f32[12,48,256]{2,1,0:T(8,128)S(1)}, u32[]{:S(2)}, u32[]{:S(2)}) %collective-permute-start.18) | collective-permute-done | bytes 589856 | tf_op jit(solution)/shard_map/ppermute | solution.py:57
  644.3 7.8 %collective-permute-done.19 = f32[12,48,256]{2,1,0:T(8,128)S(1)} collective-permute-done((f32[12,48,256]{2,1,0:T(8,128)S(1)}, f32[12,48,256]{2,1,0:T(8,128)S(1)}, u32[]{:S(2)}, u32[]{:S(2)}) %collective-permute-start.19) | collective-permute-done | bytes 589856 | tf_op jit(solution)/shard_map/ppermute | solution.py:57
  653.2 5.2 collective-permute-start.20
  666.8 8.1 %all-to-all-start.14 = ((f32[576,8,32]{0,2,1:T(8,128)}), f32[576,8,32]{0,2,1:T(8,128)}, u32[]{:S(2)}, u32[]{:S(2)}) async-start(f32[576,8,32]{0,2,1:T(8,128)} %copy.259), calls=%async_computation.14 | async-start | bytes 1310720 | tf_op jit(solution)/shard_map/all_to_all | solution.py:149
  680.8 5.4 all-to-all-done.14
  691.4 9.4 %all-to-all-done.15 = f32[576,8,32]{0,2,1:T(8,128)S(1)} async-done(((f32[576,8,32]{0,2,1:T(8,128)}), f32[576,8,32]{0,2,1:T(8,128)S(1)}, u32[]{:S(2)}, u32[]{:S(2)}) %all-to-all-start.15) | async-done | bytes 589856 | tf_op jit(solution)/shard_map/all_to_all | solution.py:149
  (299 shorter events, 259.3 us)
Async XLA Ops:
  0.0 29.2 %copy-start = (s32[32,6]{0,1:T(8,128)S(1)}, s32[32,6]{0,1:T(8,128)}, u32[]{:S(2)}) copy-start(s32[32,6]{0,1:T(8,128)} %param.6) | copy-start | bytes 2308
  18.9 16.2 %collective-permute-start = (f32[576,256]{1,0:T(8,128)}, f32[576,256]{1,0:T(8,128)}, u32[]{:S(2)}, u32[]{:S(2)}) collective-permute-start(f32[576,256]{1,0:T(8,128)} %copy.179), channel_id=1, source_target_pairs={{0,8},{8,16},{16,24},{1,9},{9,17},{17,25},{2,10},{10,18},{18,26},{... | collective-permute-start | bytes 1769480 | tf_op jit(solution)/shard_map/ppermute | solution.py:25
  23.2 16.8 %collective-permute-start.1 = (f32[576,256]{1,0:T(8,128)}, f32[576,256]{1,0:T(8,128)}, u32[]{:S(2)}, u32[]{:S(2)}) collective-permute-start(f32[576,256]{1,0:T(8,128)} %copy.179), channel_id=1, source_target_pairs={{8,0},{16,8},{24,16},{9,1},{17,9},{25,17},{10,2},{18,10},{26,18},{... | collective-permute-start | bytes 1769480 | tf_op jit(solution)/shard_map/ppermute | solution.py:26
  25.6 52.1 %all-to-all-start = ((f32[8,576,32]{1,2,0:T(8,128)}), f32[8,576,32]{1,2,0:T(8,128)S(1)}, u32[]{:S(2)}, u32[]{:S(2)}) async-start(f32[8,576,32]{1,2,0:T(8,128)} %copy.175), calls=%async_computation | async-start | bytes 1310720 | tf_op jit(solution)/shard_map/all_to_all | solution.py:80
  35.0 7.7 %collective-permute-start.2 = (f32[576,256]{1,0:T(8,128)}, f32[576,256]{1,0:T(8,128)S(1)}, u32[]{:S(2)}, u32[]{:S(2)}) collective-permute-start(f32[576,256]{1,0:T(8,128)} %collective-permute-done), channel_id=1, source_target_pairs={{8,16},{16,24},{9,17},{17,25},{10,18},{18,26},{11,19},{19,27},{12,... | collective-permute-start | bytes 1769480 | tf_op jit(solution)/shard_map/ppermute | solution.py:25
  36.4 37.3 %copy-start.49 = (pred[8,2]{1,0:T(8,128)(4,1)}, pred[8,2]{1,0:T(8,128)(4,1)S(1)}, u32[]{:S(2)}) copy-start(pred[8,2]{1,0:T(8,128)(4,1)S(1)} %copy.176) | copy-start | bytes 52
  40.0 16.2 %collective-permute-start.3 = (f32[576,256]{1,0:T(8,128)}, f32[576,256]{1,0:T(8,128)S(1)}, u32[]{:S(2)}, u32[]{:S(2)}) collective-permute-start(f32[576,256]{1,0:T(8,128)} %collective-permute-done.1), channel_id=1, source_target_pairs={{8,0},{16,8},{9,1},{17,9},{10,2},{18,10},{11,3},{19,11},{12,4},{20... | collective-permute-start | bytes 1769480 | tf_op jit(solution)/shard_map/ppermute | solution.py:26
  42.7 14.9 %collective-permute-start.4 = (f32[576,256]{1,0:T(8,128)S(1)}, f32[576,256]{1,0:T(8,128)S(1)}, u32[]{:S(2)}, u32[]{:S(2)}) collective-permute-start(f32[576,256]{1,0:T(8,128)S(1)} %collective-permute-done.2), channel_id=1, source_target_pairs={{16,24},{17,25},{18,26},{19,27},{20,28},{21,29},{22,30},{23,31}} | collective-permute-start | bytes 1769480 | tf_op jit(solution)/shard_map/ppermute | solution.py:25
  56.2 14.9 %collective-permute-start.5 = (f32[576,256]{1,0:T(8,128)S(1)}, f32[576,256]{1,0:T(8,128)S(1)}, u32[]{:S(2)}, u32[]{:S(2)}) collective-permute-start(f32[576,256]{1,0:T(8,128)S(1)} %collective-permute-done.3), channel_id=1, source_target_pairs={{8,0},{9,1},{10,2},{11,3},{12,4},{13,5},{14,6},{15,7}} | collective-permute-start | bytes 1769480 | tf_op jit(solution)/shard_map/ppermute | solution.py:26
  77.7 42.4 %all-to-all-start.2 = ((f32[8,2,4,48,256]{4,3,2,1,0:T(8,128)}), f32[8,2,4,48,256]{4,3,2,1,0:T(8,128)}, u32[]{:S(2)}, u32[]{:S(2)}) async-start(f32[8,2,4,48,256]{4,3,2,1,0:T(8,128)} %broadcast_select_fusion.5), calls=%async_computation.2 | async-start | bytes 6291456 | tf_op jit(solution)/shard_map/all_to_all | solution.py:10
  84.3 17.7 %collective-permute-start.7 = (f32[576,256]{1,0:T(8,128)}, f32[576,256]{1,0:T(8,128)S(1)}, u32[]{:S(2)}, u32[]{:S(2)}) collective-permute-start(f32[576,256]{1,0:T(8,128)} %copy.183), channel_id=1, source_target_pairs={{8,0},{16,8},{24,16},{9,1},{17,9},{25,17},{10,2},{18,10},{26,18},{... | collective-permute-start | bytes 1769480 | tf_op jit(solution)/shard_map/ppermute | solution.py:26
  85.6 17.7 %collective-permute-start.6 = (f32[576,256]{1,0:T(8,128)}, f32[576,256]{1,0:T(8,128)S(1)}, u32[]{:S(2)}, u32[]{:S(2)}) collective-permute-start(f32[576,256]{1,0:T(8,128)} %copy.182), channel_id=1, source_target_pairs={{0,8},{8,16},{16,24},{1,9},{9,17},{17,25},{2,10},{10,18},{18,26},{... | collective-permute-start | bytes 1769480 | tf_op jit(solution)/shard_map/ppermute | solution.py:25
  97.5 29.8 %copy-start.54 = (pred[8,2]{0,1:T(4,128)(4,1)S(1)}, pred[8,2]{0,1:T(4,128)(4,1)}, u32[]{:S(2)}) copy-start(pred[8,2]{0,1:T(4,128)(4,1)} %get-tuple-element.78) | copy-start | bytes 52
  102.0 24.0 %copy-start.42 = (f32[576,256]{1,0:T(8,128)}, f32[576,256]{1,0:T(8,128)S(1)}, u32[]{:S(2)}) copy-start(f32[576,256]{1,0:T(8,128)S(1)} %collective-permute-done.7) | copy-start | bytes 1769476
  103.3 21.2 %copy-start.44 = (f32[576,256]{1,0:T(8,128)}, f32[576,256]{1,0:T(8,128)S(1)}, u32[]{:S(2)}) copy-start(f32[576,256]{1,0:T(8,128)S(1)} %collective-permute-done.6) | copy-start | bytes 1769476
  120.1 42.4 %all-to-all-start.3 = ((f32[8,2,4,48,256]{4,3,2,1,0:T(8,128)}), f32[8,2,4,48,256]{4,3,2,1,0:T(8,128)}, u32[]{:S(2)}, u32[]{:S(2)}) async-start(f32[8,2,4,48,256]{4,3,2,1,0:T(8,128)} %broadcast_select_fusion.4), calls=%async_computation.3 | async-start | bytes 6291456 | tf_op jit(solution)/shard_map/all_to_all | solution.py:10
  124.6 11.8 %collective-permute-start.8 = (f32[576,256]{1,0:T(8,128)S(1)}, f32[576,256]{1,0:T(8,128)}, u32[]{:S(2)}, u32[]{:S(2)}) collective-permute-start(f32[576,256]{1,0:T(8,128)S(1)} %collective-permute-done.6), channel_id=1, source_target_pairs={{8,16},{16,24},{9,17},{17,25},{10,18},{18,26},{11,19},{19,27},{12,... | collective-permute-start | bytes 1769480 | tf_op jit(solution)/shard_map/ppermute | solution.py:25
  126.1 17.6 %collective-permute-start.9 = (f32[576,256]{1,0:T(8,128)S(1)}, f32[576,256]{1,0:T(8,128)}, u32[]{:S(2)}, u32[]{:S(2)}) collective-permute-start(f32[576,256]{1,0:T(8,128)S(1)} %collective-permute-done.7), channel_id=1, source_target_pairs={{8,0},{16,8},{9,1},{17,9},{10,2},{18,10},{11,3},{19,11},{12,4},{20... | collective-permute-start | bytes 1769480 | tf_op jit(solution)/shard_map/ppermute | solution.py:26
  162.5 41.5 %all-to-all-start.4 = ((f32[8,2,4,48,256]{4,3,2,1,0:T(8,128)}), f32[8,2,4,48,256]{4,3,2,1,0:T(8,128)S(1)}, u32[]{:S(2)}, u32[]{:S(2)}) async-start(f32[8,2,4,48,256]{4,3,2,1,0:T(8,128)} %broadcast_select_fusion.3), calls=%async_computation.4 | async-start | bytes 6291456 | tf_op jit(solution)/shard_map/all_to_all | solution.py:10
  169.5 4.3 collective-permute-start.10
  170.2 17.9 %collective-permute-start.11 = (f32[576,256]{1,0:T(8,128)}, f32[576,256]{1,0:T(8,128)}, u32[]{:S(2)}, u32[]{:S(2)}) collective-permute-start(f32[576,256]{1,0:T(8,128)} %collective-permute-done.9), channel_id=1, source_target_pairs={{8,0},{9,1},{10,2},{11,3},{12,4},{13,5},{14,6},{15,7}} | collective-permute-start | bytes 1769480 | tf_op jit(solution)/shard_map/ppermute | solution.py:26
  216.3 42.3 %all-to-all-start.9 = ((f32[8,2,4,48,256]{4,3,2,1,0:T(8,128)}), f32[8,2,4,48,256]{4,3,2,1,0:T(8,128)}, u32[]{:S(2)}, u32[]{:S(2)}) async-start(f32[8,2,4,48,256]{4,3,2,1,0:T(8,128)} %broadcast_select_fusion), calls=%async_computation.9 | async-start | bytes 6291456 | tf_op jit(solution)/shard_map/all_to_all | solution.py:10
  258.7 42.6 %all-to-all-start.7 = ((f32[8,2,4,48,256]{4,3,2,1,0:T(8,128)}), f32[8,2,4,48,256]{4,3,2,1,0:T(8,128)}, u32[]{:S(2)}, u32[]{:S(2)}) async-start(f32[8,2,4,48,256]{4,3,2,1,0:T(8,128)} %broadcast_select_fusion.1), calls=%async_computation.7 | async-start | bytes 6291456 | tf_op jit(solution)/shard_map/all_to_all | solution.py:10
  301.2 43.2 %all-to-all-start.5 = ((f32[8,2,4,48,256]{4,3,2,1,0:T(8,128)}), f32[8,2,4,48,256]{4,3,2,1,0:T(8,128)}, u32[]{:S(2)}, u32[]{:S(2)}) async-start(f32[8,2,4,48,256]{4,3,2,1,0:T(8,128)} %broadcast_select_fusion.2), calls=%async_computation.5 | async-start | bytes 6291456 | tf_op jit(solution)/shard_map/all_to_all | solution.py:10
  344.4 42.5 %all-to-all-start.10 = ((f32[8,2,4,48,256]{4,3,2,1,0:T(8,128)}), f32[8,2,4,48,256]{4,3,2,1,0:T(8,128)}, u32[]{:S(2)}, u32[]{:S(2)}) async-start(f32[8,2,4,48,256]{4,3,2,1,0:T(8,128)} %copy.212), calls=%async_computation.10 | async-start | bytes 6291456 | tf_op jit(solution)/shard_map/all_to_all | solution.py:10
  386.9 42.6 %all-to-all-start.6 = ((f32[8,2,4,48,256]{4,3,2,1,0:T(8,128)}), f32[8,2,4,48,256]{4,3,2,1,0:T(8,128)}, u32[]{:S(2)}, u32[]{:S(2)}) async-start(f32[8,2,4,48,256]{4,3,2,1,0:T(8,128)} %copy.196), calls=%async_computation.6 | async-start | bytes 6291456 | tf_op jit(solution)/shard_map/all_to_all | solution.py:10
  429.5 42.4 %all-to-all-start.8 = ((f32[8,2,4,48,256]{4,3,2,1,0:T(8,128)}), f32[8,2,4,48,256]{4,3,2,1,0:T(8,128)}, u32[]{:S(2)}, u32[]{:S(2)}) async-start(f32[8,2,4,48,256]{4,3,2,1,0:T(8,128)} %copy.204), calls=%async_computation.8 | async-start | bytes 6291456 | tf_op jit(solution)/shard_map/all_to_all | solution.py:10
  483.5 42.5 %all-to-all-start.11 = ((f32[8,2,4,48,256]{4,3,2,1,0:T(8,128)}), f32[8,2,4,48,256]{4,3,2,1,0:T(8,128)}, u32[]{:S(2)}, u32[]{:S(2)}) async-start(f32[8,2,4,48,256]{4,3,2,1,0:T(8,128)} %copy.219), calls=%async_computation.11 | async-start | bytes 6291456 | tf_op jit(solution)/shard_map/all_to_all | solution.py:10
  496.4 10.1 %collective-permute-start.13 = (f32[12,48,256]{2,1,0:T(8,128)S(1)}, f32[12,48,256]{2,1,0:T(8,128)}, u32[]{:S(2)}, u32[]{:S(2)}) collective-permute-start(f32[12,48,256]{2,1,0:T(8,128)S(1)} %copy.218), channel_id=1, source_target_pairs={{24,16},{25,17},{26,18},{27,19},{28,20},{29,21},{30,22},{31,23}} | collective-permute-start | bytes 1769480 | tf_op jit(solution)/shard_map/ppermute | solution.py:58
  497.9 14.6 %collective-permute-start.12 = (f32[12,48,256]{2,1,0:T(8,128)S(1)}, f32[12,48,256]{2,1,0:T(8,128)}, u32[]{:S(2)}, u32[]{:S(2)}) collective-permute-start(f32[12,48,256]{2,1,0:T(8,128)S(1)} %copy.217), channel_id=1, source_target_pairs={{0,8},{1,9},{2,10},{3,11},{4,12},{5,13},{6,14},{7,15}} | collective-permute-start | bytes 1769480 | tf_op jit(solution)/shard_map/ppermute | solution.py:57
  504.4 21.6 %copy-start.7 = (f32[4,48,256,12]{2,3,1,0:T(8,128)S(1)}, f32[4,48,256,12]{2,3,1,0:T(8,128)}, u32[]{:S(2)}) copy-start(f32[4,48,256,12]{2,3,1,0:T(8,128)} %copy-done.6) | copy-start | bytes 7077892
  531.4 42.6 %all-to-all-start.12 = ((f32[8,2,4,48,256]{4,3,2,1,0:T(8,128)}), f32[8,2,4,48,256]{4,3,2,1,0:T(8,128)}, u32[]{:S(2)}, u32[]{:S(2)}) async-start(f32[8,2,4,48,256]{4,3,2,1,0:T(8,128)} %copy.224), calls=%async_computation.12 | async-start | bytes 6291456 | tf_op jit(solution)/shard_map/all_to_all | solution.py:10
  544.0 9.7 %collective-permute-start.15 = (f32[12,48,256]{2,1,0:T(8,128)S(1)}, f32[12,48,256]{2,1,0:T(8,128)}, u32[]{:S(2)}, u32[]{:S(2)}) collective-permute-start(f32[12,48,256]{2,1,0:T(8,128)S(1)} %copy.223), channel_id=1, source_target_pairs={{16,8},{24,16},{17,9},{25,17},{18,10},{26,18},{19,11},{27,19},{20,... | collective-permute-start | bytes 1769480 | tf_op jit(solution)/shard_map/ppermute | solution.py:58
  545.5 14.7 %collective-permute-start.14 = (f32[12,48,256]{2,1,0:T(8,128)S(1)}, f32[12,48,256]{2,1,0:T(8,128)}, u32[]{:S(2)}, u32[]{:S(2)}) collective-permute-start(f32[12,48,256]{2,1,0:T(8,128)S(1)} %copy.222), channel_id=1, source_target_pairs={{0,8},{8,16},{1,9},{9,17},{2,10},{10,18},{3,11},{11,19},{4,12},{12... | collective-permute-start | bytes 1769480 | tf_op jit(solution)/shard_map/ppermute | solution.py:57
  551.7 22.3 %copy-start.8 = (f32[4,48,256,12]{2,3,1,0:T(8,128)S(1)}, f32[4,48,256,12]{2,3,1,0:T(8,128)}, u32[]{:S(2)}) copy-start(f32[4,48,256,12]{2,3,1,0:T(8,128)} %copy-done.6) | copy-start | bytes 7077892
  579.4 41.5 %all-to-all-start.13 = ((f32[8,2,4,48,256]{4,3,2,1,0:T(8,128)}), f32[8,2,4,48,256]{4,3,2,1,0:T(8,128)S(1)}, u32[]{:S(2)}, u32[]{:S(2)}) async-start(f32[8,2,4,48,256]{4,3,2,1,0:T(8,128)} %copy.229), calls=%async_computation.13 | async-start | bytes 6291456 | tf_op jit(solution)/shard_map/all_to_all | solution.py:10
  586.0 17.7 %collective-permute-start.17 = (f32[12,48,256]{2,1,0:T(8,128)S(1)}, f32[12,48,256]{2,1,0:T(8,128)S(1)}, u32[]{:S(2)}, u32[]{:S(2)}) collective-permute-start(f32[12,48,256]{2,1,0:T(8,128)S(1)} %copy.228), channel_id=1, source_target_pairs={{8,0},{16,8},{24,16},{9,1},{17,9},{25,17},{10,2},{18,10},{26,18},{... | collective-permute-start | bytes 1769480 | tf_op jit(solution)/shard_map/ppermute | solution.py:58
  587.3 17.4 %collective-permute-start.16 = (f32[12,48,256]{2,1,0:T(8,128)S(1)}, f32[12,48,256]{2,1,0:T(8,128)}, u32[]{:S(2)}, u32[]{:S(2)}) collective-permute-start(f32[12,48,256]{2,1,0:T(8,128)S(1)} %copy.227), channel_id=1, source_target_pairs={{0,8},{8,16},{16,24},{1,9},{9,17},{17,25},{2,10},{10,18},{18,26},{... | collective-permute-start | bytes 1769480 | tf_op jit(solution)/shard_map/ppermute | solution.py:57
  627.0 11.3 %collective-permute-start.18 = (f32[12,48,256]{2,1,0:T(8,128)S(1)}, f32[12,48,256]{2,1,0:T(8,128)S(1)}, u32[]{:S(2)}, u32[]{:S(2)}) collective-permute-start(f32[12,48,256]{2,1,0:T(8,128)S(1)} %copy.236), channel_id=1, source_target_pairs={{0,8},{1,9},{2,10},{3,11},{4,12},{5,13},{6,14},{7,15}} | collective-permute-start | bytes 1769480 | tf_op jit(solution)/shard_map/ppermute | solution.py:57
  628.8 14.4 %collective-permute-start.21 = (f32[12,48,256]{2,1,0:T(8,128)S(1)}, f32[12,48,256]{2,1,0:T(8,128)S(1)}, u32[]{:S(2)}, u32[]{:S(2)}) collective-permute-start(f32[12,48,256]{2,1,0:T(8,128)S(1)} %copy.239), channel_id=1, source_target_pairs={{24,16},{25,17},{26,18},{27,19},{28,20},{29,21},{30,22},{31,23}} | collective-permute-start | bytes 1769480 | tf_op jit(solution)/shard_map/ppermute | solution.py:58
  638.6 22.6 %copy-start.37 = (f32[1,48,256,12]{2,3,1,0:T(8,128)S(1)}, f32[1,48,256,12]{2,3,1,0:T(8,128)}, u32[]{:S(2)}) copy-start(f32[1,48,256,12]{2,3,1,0:T(8,128)} %get-tuple-element.84) | copy-start | bytes 1769476
  638.6 22.6 %copy-start.41 = (f32[12,48,256]{2,1,0:T(8,128)S(1)}, f32[12,48,256]{2,1,0:T(8,128)}, u32[]{:S(2)}) copy-start(f32[12,48,256]{2,1,0:T(8,128)} %copy-done.40) | copy-start | bytes 1769476
  638.6 13.4 %collective-permute-start.19 = (f32[12,48,256]{2,1,0:T(8,128)S(1)}, f32[12,48,256]{2,1,0:T(8,128)S(1)}, u32[]{:S(2)}, u32[]{:S(2)}) collective-permute-start(f32[12,48,256]{2,1,0:T(8,128)S(1)} %fusion.24), channel_id=1, source_target_pairs={{0,8},{8,16},{1,9},{9,17},{2,10},{10,18},{3,11},{11,19},{4,12},{12... | collective-permute-start | bytes 1769480 | tf_op jit(solution)/shard_map/ppermute | solution.py:57
  643.6 14.9 %collective-permute-start.22 = (f32[12,48,256]{2,1,0:T(8,128)S(1)}, f32[12,48,256]{2,1,0:T(8,128)S(1)}, u32[]{:S(2)}, u32[]{:S(2)}) collective-permute-start(f32[12,48,256]{2,1,0:T(8,128)S(1)} %fusion.22), channel_id=1, source_target_pairs={{16,8},{24,16},{17,9},{25,17},{18,10},{26,18},{19,11},{27,19},{20,... | collective-permute-start | bytes 1769480 | tf_op jit(solution)/shard_map/ppermute | solution.py:58
  653.2 21.7 %collective-permute-start.20 = (f32[12,48,256]{2,1,0:T(8,128)}, f32[12,48,256]{2,1,0:T(8,128)}, u32[]{:S(2)}, u32[]{:S(2)}) collective-permute-start(f32[12,48,256]{2,1,0:T(8,128)} %fusion.23), channel_id=1, source_target_pairs={{0,8},{8,16},{16,24},{1,9},{9,17},{17,25},{2,10},{10,18},{18,26},{... | collective-permute-start | bytes 1769480 | tf_op jit(solution)/shard_map/ppermute | solution.py:57
  659.6 15.3 %collective-permute-start.23 = (f32[12,48,256]{2,1,0:T(8,128)}, f32[12,48,256]{2,1,0:T(8,128)}, u32[]{:S(2)}, u32[]{:S(2)}) collective-permute-start(f32[12,48,256]{2,1,0:T(8,128)} %fusion.21), channel_id=1, source_target_pairs={{8,0},{16,8},{24,16},{9,1},{17,9},{25,17},{10,2},{18,10},{26,18},{... | collective-permute-start | bytes 1769480 | tf_op jit(solution)/shard_map/ppermute | solution.py:58
  666.8 19.3 %all-to-all-start.14 = ((f32[576,8,32]{0,2,1:T(8,128)}), f32[576,8,32]{0,2,1:T(8,128)}, u32[]{:S(2)}, u32[]{:S(2)}) async-start(f32[576,8,32]{0,2,1:T(8,128)} %copy.259), calls=%async_computation.14 | async-start | bytes 1310720 | tf_op jit(solution)/shard_map/all_to_all | solution.py:149
  686.2 14.6 %all-to-all-start.15 = ((f32[576,8,32]{0,2,1:T(8,128)}), f32[576,8,32]{0,2,1:T(8,128)S(1)}, u32[]{:S(2)}, u32[]{:S(2)}) async-start(f32[576,8,32]{0,2,1:T(8,128)} %copy.260), calls=%async_computation.15 | async-start | bytes 1310720 | tf_op jit(solution)/shard_map/all_to_all | solution.py:149
  (53 other events, 358.6 us)
where the time goes:
time: 712 us; the launch traced here: 703 us
  waiting for transfers between devices  240 us (34%)
  local copies, waits for them, and re-layouts  151 us (21%)
  matrix products  128 us (18%)
  starting transfers between devices  117 us (16%)
  other arithmetic  45.7 us (6%)
  blocking collectives  16.1 us (2%)
    all_to_all x12, waiting for transfers between devices, band_exchange(): lax.all_to_all(outgoing, 'band', split_axis=0, concat_axis=0, tiled=True)  137 us
    all_to_all x12, starting transfers between devices, band_exchange(): lax.all_to_all(outgoing, 'band', split_axis=0, concat_axis=0, tiled=True)  53.2 us
    dot_general x6, matrix products, body(): jnp.dot(r[0], r[1].T, precision=PRECISION, preferred_element_type=jnp.flo...  52.3 us
    ppermute x6, waiting for transfers between devices, line_gather(): lax.ppermute(leftward, axis, [(i + 1, i) for i in range(0, count - step)])  51.8 us
    dot_general x6, matrix products, body(): jnp.dot(kernel, rows[h][1], precision=PRECISION, preferred_element_type=j...  43.4 us
    ppermute x6, waiting for transfers between devices, line_reduce(): lax.ppermute(send_right, axis, [(i, i + 1) for i in range(0, step)])  29.1 us
    dot_general x3, local copies, waits for them, and re-layouts, body(): jnp.dot(kernel.T, rows[h][0], precision=PRECISION, preferred_element_type...  28.9 us
    dot_general x6, matrix products, body(): jnp.dot(kernel.T, rows[h][0], precision=PRECISION, preferred_element_type...  27.7 us
  transfers between devices with their start and end apart: 39, of which 26 were waited for; matrix products, arithmetic and copies ran while one was open for 38% of the time, Pallas kernels for 0%

commit v1 on v0

--- a/solution.py
+++ b/solution.py
@@ -4,6 +4,35 @@
 from jax.sharding import PartitionSpec as P
 
 PRECISION = lax.Precision.HIGH
+
+
+def _attach_works(u_in, dim_no, z_in):
+    g_now = u_in.shape
+    val2 = u_in.reshape(*g_now[:dim_no], z_in, g_now[dim_no] // z_in, *g_now[dim_no + 1 :])
+    return jnp.moveaxis(val2, dim_no, 0)
+
+
+def load_side_on(array_here, axis_no):
+    item_now = list(array_here.shape[1:])
+    item_now[axis_no] *= array_here.shape[0]
+    return jnp.moveaxis(array_here, 0, axis_no).reshape(item_now)
+
+
+def check_the_run(s0, row_axis, inputs, array_in):
+    carry = jax.lax.axis_size(row_axis)
+    tmp = jax.lax.axis_index(row_axis)
+    block_out, carry_in = (carry, tmp)
+    passed = _attach_works(s0, inputs, block_out)
+    column = [passed[carry_in]]
+    for jj in range(1, block_out):
+        earlier = passed[carry_in ^ jj]
+        reached = jax.lax.ppermute(
+            earlier, axis_name=row_axis, perm=[(pp, pp ^ jj) for pp in range(block_out)]
+        )
+        column.append(reached)
+    small = jnp.stack(column, axis=0)
+    passed = small[carry_in ^ jnp.arange(block_out)]
+    return load_side_on(passed, array_in)
 
 
 def band_exchange(outgoing):
@@ -146,13 +175,7 @@
     first_home, second_returned = line_reduce(sum_blocks(returned[0]), "grp", group_count, held)
     second_home, _ = line_reduce(sum_blocks(second_returned), "grp", group_count)
     home = [
-        lax.all_to_all(
-            rows.reshape(block_count * piece_rows, half),
-            "band",
-            split_axis=1,
-            concat_axis=0,
-            tiled=True,
-        )
+        check_the_run(rows.reshape(block_count * piece_rows, half), "band", 1, 0)
         for rows in (first_home, second_home)
     ]
     return jnp.concatenate(home, axis=1)

time: 712 us -> 756 us (1.062)
  local copies, waits for them, and re-layouts: 151 us -> 182 us
  starting transfers between devices: 117 us -> 128 us
    ppermute x0 -> x14, starting transfers between devices: none -> 22.4 us  [check_the_run(): jax.lax.ppermute(earlier, axis_name=row_axis, perm=[(pp, pp ^ jj) for pp...]
    unnamed x124 -> x162, local copies, waits for them, and re-layouts: 13.9 us -> 33 us
    another operation x4 -> x9, local copies, waits for them, and re-layouts: 2.58 us -> 21.3 us
    all_to_all x2 -> x0, waiting for transfers between devices: 14.8 us -> none  [body(): lax.all_to_all(rows.reshape(block_count * piece_rows, half), 'band', spli...]
    all_to_all x2 -> x0, starting transfers between devices: 11.6 us -> none  [body(): lax.all_to_all(rows.reshape(block_count * piece_rows, half), 'band', spli...]
    ppermute x0 -> x14, waiting for transfers between devices: none -> 9.02 us  [check_the_run(): jax.lax.ppermute(earlier, axis_name=row_axis, perm=[(pp, pp ^ jj) for pp...]
    all_to_all x8 -> x0, local copies, waits for them, and re-layouts: 8.82 us -> none  [body(): lax.all_to_all(rows.reshape(block_count * piece_rows, half), 'band', spli...]
  transfers between devices with their start and end apart: 39 -> 51, of which waited for: 26 -> 30; matrix products, arithmetic and copies ran while one was open for 38% -> 36% of each run, Pallas kernels for 0% -> 0%
where the time goes in v1:
time: 756 us; the launch traced here: 746 us
  waiting for transfers between devices  241 us (32%)
  local copies, waits for them, and re-layouts  182 us (24%)
  starting transfers between devices  128 us (17%)
  matrix products  128 us (17%)
  other arithmetic  45.8 us (6%)
  blocking collectives  16.1 us (2%)
    all_to_all x12, waiting for transfers between devices, band_exchange(): lax.all_to_all(outgoing, 'band', split_axis=0, concat_axis=0, tiled=True)  137 us
    all_to_all x12, starting transfers between devices, band_exchange(): lax.all_to_all(outgoing, 'band', split_axis=0, concat_axis=0, tiled=True)  53.2 us
    dot_general x6, matrix products, body(): jnp.dot(r[0], r[1].T, precision=PRECISION, preferred_element_type=jnp.flo...  52.3 us
    ppermute x6, waiting for transfers between devices, line_gather(): lax.ppermute(leftward, axis, [(i + 1, i) for i in range(0, count - step)])  52 us
    dot_general x6, matrix products, body(): jnp.dot(kernel, rows[h][1], precision=PRECISION, preferred_element_type=j...  43.4 us
    unnamed x162, local copies, waits for them, and re-layouts  33 us
    ppermute x6, waiting for transfers between devices, line_reduce(): lax.ppermute(send_right, axis, [(i, i + 1) for i in range(0, step)])  29.6 us
    dot_general x3, local copies, waits for them, and re-layouts, body(): jnp.dot(kernel.T, rows[h][0], precision=PRECISION, preferred_element_type...  29 us
  transfers between devices with their start and end apart: 51, of which 30 were waited for; matrix products, arithmetic and copies ran while one was open for 36% of the time, Pallas kernels for 0%

profile of v1, /device:TPU:0, one launch (start us, length us, event | category | flops | bytes accessed | tf_op | source)
XLA Modules:
  0.0 746.2 jit_solution(11628895938565403924)
XLA Ops:
  1.7 16.1 %all_to_all.98 = f32[8,576,32]{1,2,0:T(8,128)S(1)} all-to-all(f32[8,576,32]{1,2,0:T(8,128)S(1)} %copy.177), channel_id=1, replica_groups=mesh['grp'=4,'band'=8] {'band'}, dimensions={0} | all-to-all | bytes 1179648 | tf_op jit(solution)/shard_map/all_to_all | solution.py:109
  29.2 5.8 collective-permute-done
  44.5 11.7 %collective-permute-done.3 = f32[576,256]{1,0:T(8,128)S(1)} collective-permute-done((f32[576,256]{1,0:T(8,128)}, f32[576,256]{1,0:T(8,128)S(1)}, u32[]{:S(2)}, u32[]{:S(2)}) %collective-permute-start.3) | collective-permute-done | bytes 589856 | tf_op jit(solution)/shard_map/ppermute | solution.py:55
  57.6 13.5 %collective-permute-done.5 = f32[576,256]{1,0:T(8,128)S(1)} collective-permute-done((f32[576,256]{1,0:T(8,128)S(1)}, f32[576,256]{1,0:T(8,128)S(1)}, u32[]{:S(2)}, u32[]{:S(2)}) %collective-permute-start.5) | collective-permute-done | bytes 589856 | tf_op jit(solution)/shard_map/ppermute | solution.py:55
  103.4 16.7 %all-to-all-done.2 = f32[8,2,4,48,256]{4,3,2,1,0:T(8,128)} async-done(((f32[8,2,4,48,256]{4,3,2,1,0:T(8,128)}), f32[8,2,4,48,256]{4,3,2,1,0:T(8,128)}, u32[]{:S(2)}, u32[]{:S(2)}) %all-to-all-start.2) | async-done | bytes 3145760 | tf_op jit(solution)/shard_map/all_to_all | solution.py:39
  136.3 7.4 collective-permute-done.9
  143.7 18.8 %all-to-all-done.3 = f32[8,2,4,48,256]{4,3,2,1,0:T(8,128)} async-done(((f32[8,2,4,48,256]{4,3,2,1,0:T(8,128)}), f32[8,2,4,48,256]{4,3,2,1,0:T(8,128)}, u32[]{:S(2)}, u32[]{:S(2)}) %all-to-all-start.3) | async-done | bytes 3145760 | tf_op jit(solution)/shard_map/all_to_all | solution.py:39
  176.3 11.8 %collective-permute-done.11 = f32[576,256]{1,0:T(8,128)} collective-permute-done((f32[576,256]{1,0:T(8,128)}, f32[576,256]{1,0:T(8,128)}, u32[]{:S(2)}, u32[]{:S(2)}) %collective-permute-start.11) | collective-permute-done | bytes 589856 | tf_op jit(solution)/shard_map/ppermute | solution.py:55
  188.1 15.8 %all-to-all-done.4 = f32[8,2,4,48,256]{4,3,2,1,0:T(8,128)S(1)} async-done(((f32[8,2,4,48,256]{4,3,2,1,0:T(8,128)}), f32[8,2,4,48,256]{4,3,2,1,0:T(8,128)S(1)}, u32[]{:S(2)}, u32[]{:S(2)}) %all-to-all-start.4) | async-done | bytes 3145760 | tf_op jit(solution)/shard_map/all_to_all | solution.py:39
  231.8 27.0 %all-to-all-done.9 = f32[8,2,4,48,256]{4,3,2,1,0:T(8,128)} async-done(((f32[8,2,4,48,256]{4,3,2,1,0:T(8,128)}), f32[8,2,4,48,256]{4,3,2,1,0:T(8,128)}, u32[]{:S(2)}, u32[]{:S(2)}) %all-to-all-start.9) | async-done | bytes 3145760 | tf_op jit(solution)/shard_map/all_to_all | solution.py:39
  258.7 4.7 all-to-all-start.7
  265.9 6.4 fusion.45
  276.3 6.3 fusion.46
  291.2 6.4 fusion.47
  301.3 4.9 all-to-all-start.5
  312.0 9.6 %fusion = f32[1536,1536]{1,0:T(8,128)} fusion(f32[1536,1536]{1,0:T(8,128)S(1)} %copy-done.5, f32[1536,256]{1,0:T(8,128)S(1)} %bitcast.387, f32[1536,256]{1,0:T(8,128)S(1)} %bitcast.389, f32[3,1536,1536]{2,1,0:T(8,128)} %param.7, f32[]{:T(128)} %bitcast.81), kind=kOutput, calls=%fused_computation.9 | convolution fusion | flops 3630956544 | bytes 31457284 | tf_op jit(solution)/shard_map/dot_general | solution.py:149
  321.6 9.7 %copy.211 = f32[1536,1536]{1,0:T(8,128)} copy(f32[1536,1536]{0,1:T(8,128)} %bitcast.356) | data formatting | bytes 18874368 | tf_op jit(solution)/shard_map/dot_general | solution.py:159
  331.2 7.0 convolution_bitcast_fusion.7
  344.6 4.6 all-to-all-start.10
  351.7 12.1 %fusion.2 = f32[1536,1536]{1,0:T(8,128)} fusion(f32[1536,1536]{1,0:T(8,128)} %fusion.45, f32[1536,256]{1,0:T(8,128)S(1)} %bitcast.397, f32[1536,256]{1,0:T(8,128)S(1)} %bitcast.395, f32[3,1536,1536]{2,1,0:T(8,128)} %param.7, f32[]{:T(128)} %bitcast.39), kind=kOutput, calls=%fused_computation.13 | convolution fusion | flops 3630956544 | bytes 31457284 | tf_op jit(solution)/shard_map/dot_general | solution.py:149
  363.8 9.7 %copy.195 = f32[1536,1536]{1,0:T(8,128)} copy(f32[1536,1536]{0,1:T(8,128)} %bitcast.362) | data formatting | bytes 18874368 | tf_op jit(solution)/shard_map/dot_general | solution.py:159
  373.5 7.0 convolution_bitcast_fusion.11
  387.1 4.7 all-to-all-start.6
  394.2 11.4 %fusion.1 = f32[1536,1536]{1,0:T(8,128)} fusion(f32[1536,1536]{1,0:T(8,128)} %fusion.46, f32[1536,256]{1,0:T(8,128)S(1)} %bitcast.391, f32[1536,256]{1,0:T(8,128)S(1)} %bitcast.393, f32[3,1536,1536]{2,1,0:T(8,128)} %param.7, f32[]{:T(128)} %bitcast.60), kind=kOutput, calls=%fused_computation.11 | convolution fusion | flops 3630956544 | bytes 31457284 | tf_op jit(solution)/shard_map/dot_general | solution.py:149
  405.6 9.6 %copy.203 = f32[1536,1536]{1,0:T(8,128)} copy(f32[1536,1536]{0,1:T(8,128)} %bitcast.359) | data formatting | bytes 18874368 | tf_op jit(solution)/shard_map/dot_general | solution.py:159
  415.3 7.4 convolution_bitcast_fusion.9
  434.2 7.4 convolution_bitcast_fusion.5
  441.6 7.3 convolution_bitcast_fusion.4
  451.0 5.4 copy.215
  456.4 5.4 copy.213
  461.7 10.3 %all-to-all-done.8 = f32[8,2,4,48,256]{4,3,2,1,0:T(8,128)} async-done(((f32[8,2,4,48,256]{4,3,2,1,0:T(8,128)}), f32[8,2,4,48,256]{4,3,2,1,0:T(8,128)}, u32[]{:S(2)}, u32[]{:S(2)}) %all-to-all-start.8) | async-done | bytes 3145760 | tf_op jit(solution)/shard_map/all_to_all | solution.py:39
  488.4 7.5 convolution_bitcast_fusion.3
  506.7 6.0 collective-permute-done.12
  512.7 13.5 %all-to-all-done.11 = f32[8,2,4,48,256]{4,3,2,1,0:T(8,128)} async-done(((f32[8,2,4,48,256]{4,3,2,1,0:T(8,128)}), f32[8,2,4,48,256]{4,3,2,1,0:T(8,128)}, u32[]{:S(2)}, u32[]{:S(2)}) %all-to-all-start.11) | async-done | bytes 3145760 | tf_op jit(solution)/shard_map/all_to_all | solution.py:39
  531.6 4.7 all-to-all-start.12
  536.4 7.0 convolution_bitcast_fusion.1
  554.0 6.3 collective-permute-done.14
  560.3 13.9 %all-to-all-done.12 = f32[8,2,4,48,256]{4,3,2,1,0:T(8,128)} async-done(((f32[8,2,4,48,256]{4,3,2,1,0:T(8,128)}), f32[8,2,4,48,256]{4,3,2,1,0:T(8,128)}, u32[]{:S(2)}, u32[]{:S(2)}) %all-to-all-start.12) | async-done | bytes 3145760 | tf_op jit(solution)/shard_map/all_to_all | solution.py:39
  587.6 5.6 collective-permute-start.16
  593.2 5.4 copy.232
  598.6 5.4 copy.233
  605.0 16.1 %all-to-all-done.13 = f32[8,2,4,48,256]{4,3,2,1,0:T(8,128)S(1)} async-done(((f32[8,2,4,48,256]{4,3,2,1,0:T(8,128)}), f32[8,2,4,48,256]{4,3,2,1,0:T(8,128)S(1)}, u32[]{:S(2)}, u32[]{:S(2)}) %all-to-all-start.13) | async-done | bytes 3145760 | tf_op jit(solution)/shard_map/all_to_all | solution.py:39
  629.8 8.7 %collective-permute-done.25 = f32[12,48,256]{2,1,0:T(8,128)S(1)} collective-permute-done((f32[12,48,256]{2,1,0:T(8,128)S(1)}, f32[12,48,256]{2,1,0:T(8,128)S(1)}, u32[]{:S(2)}, u32[]{:S(2)}) %collective-permute-start.25) | collective-permute-done | bytes 589856 | tf_op jit(solution)/shard_map/ppermute | solution.py:86
  644.5 7.6 %collective-permute-done.26 = f32[12,48,256]{2,1,0:T(8,128)S(1)} collective-permute-done((f32[12,48,256]{2,1,0:T(8,128)S(1)}, f32[12,48,256]{2,1,0:T(8,128)S(1)}, u32[]{:S(2)}, u32[]{:S(2)}) %collective-permute-start.26) | collective-permute-done | bytes 589856 | tf_op jit(solution)/shard_map/ppermute | solution.py:86
  653.3 5.2 collective-permute-start.27
  666.0 6.1 collective-permute-done.30
  677.5 13.3 %constant_dynamic-slice_fusion = (f32[576,1,32]{2,1,0:T(1,128)}, f32[576,1,32]{2,1,0:T(1,128)}, f32[576,1,32]{2,1,0:T(1,128)}, f32[576,1,32]{2,1,0:T(1,128)}, f3...) fusion(f32[576,8,32]{2,1,0:T(8,128)} %reshape.348, ...), kind=kLoop, calls=%fused_computation.107 | loop fusion | bytes 2359328 | tf_op jit(solution)/shard_map/dynamic-slice.29
  701.8 5.5 collective-permute-start.24
  (366 shorter events, 300.4 us)
Async XLA Ops:
  18.8 16.2 %collective-permute-start = (f32[576,256]{1,0:T(8,128)}, f32[576,256]{1,0:T(8,128)}, u32[]{:S(2)}, u32[]{:S(2)}) collective-permute-start(f32[576,256]{1,0:T(8,128)} %copy.179), channel_id=1, source_target_pairs={{0,8},{8,16},{16,24},{1,9},{9,17},{17,25},{2,10},{10,18},{18,26},{... | collective-permute-start | bytes 1769480 | tf_op jit(solution)/shard_map/ppermute | solution.py:54
  23.1 16.8 %collective-permute-start.1 = (f32[576,256]{1,0:T(8,128)}, f32[576,256]{1,0:T(8,128)}, u32[]{:S(2)}, u32[]{:S(2)}) collective-permute-start(f32[576,256]{1,0:T(8,128)} %copy.179), channel_id=1, source_target_pairs={{8,0},{16,8},{24,16},{9,1},{17,9},{25,17},{10,2},{18,10},{26,18},{... | collective-permute-start | bytes 1769480 | tf_op jit(solution)/shard_map/ppermute | solution.py:55
  25.6 52.2 %all-to-all-start = ((f32[8,576,32]{1,2,0:T(8,128)}), f32[8,576,32]{1,2,0:T(8,128)S(1)}, u32[]{:S(2)}, u32[]{:S(2)}) async-start(f32[8,576,32]{1,2,0:T(8,128)} %copy.175), calls=%async_computation | async-start | bytes 1310720 | tf_op jit(solution)/shard_map/all_to_all | solution.py:109
  35.0 7.6 %collective-permute-start.2 = (f32[576,256]{1,0:T(8,128)}, f32[576,256]{1,0:T(8,128)S(1)}, u32[]{:S(2)}, u32[]{:S(2)}) collective-permute-start(f32[576,256]{1,0:T(8,128)} %collective-permute-done), channel_id=1, source_target_pairs={{8,16},{16,24},{9,17},{17,25},{10,18},{18,26},{11,19},{19,27},{12,... | collective-permute-start | bytes 1769480 | tf_op jit(solution)/shard_map/ppermute | solution.py:54
  39.9 16.2 %collective-permute-start.3 = (f32[576,256]{1,0:T(8,128)}, f32[576,256]{1,0:T(8,128)S(1)}, u32[]{:S(2)}, u32[]{:S(2)}) collective-permute-start(f32[576,256]{1,0:T(8,128)} %collective-permute-done.1), channel_id=1, source_target_pairs={{8,0},{16,8},{9,1},{17,9},{10,2},{18,10},{11,3},{19,11},{12,4},{20... | collective-permute-start | bytes 1769480 | tf_op jit(solution)/shard_map/ppermute | solution.py:55
  42.7 14.9 %collective-permute-start.4 = (f32[576,256]{1,0:T(8,128)S(1)}, f32[576,256]{1,0:T(8,128)S(1)}, u32[]{:S(2)}, u32[]{:S(2)}) collective-permute-start(f32[576,256]{1,0:T(8,128)S(1)} %collective-permute-done.2), channel_id=1, source_target_pairs={{16,24},{17,25},{18,26},{19,27},{20,28},{21,29},{22,30},{23,31}} | collective-permute-start | bytes 1769480 | tf_op jit(solution)/shard_map/ppermute | solution.py:54
  56.2 14.9 %collective-permute-start.5 = (f32[576,256]{1,0:T(8,128)S(1)}, f32[576,256]{1,0:T(8,128)S(1)}, u32[]{:S(2)}, u32[]{:S(2)}) collective-permute-start(f32[576,256]{1,0:T(8,128)S(1)} %collective-permute-done.3), channel_id=1, source_target_pairs={{8,0},{9,1},{10,2},{11,3},{12,4},{13,5},{14,6},{15,7}} | collective-permute-start | bytes 1769480 | tf_op jit(solution)/shard_map/ppermute | solution.py:55
  77.8 42.3 %all-to-all-start.2 = ((f32[8,2,4,48,256]{4,3,2,1,0:T(8,128)}), f32[8,2,4,48,256]{4,3,2,1,0:T(8,128)}, u32[]{:S(2)}, u32[]{:S(2)}) async-start(f32[8,2,4,48,256]{4,3,2,1,0:T(8,128)} %broadcast_select_fusion.5), calls=%async_computation.2 | async-start | bytes 6291456 | tf_op jit(solution)/shard_map/all_to_all | solution.py:39
  84.4 17.7 %collective-permute-start.7 = (f32[576,256]{1,0:T(8,128)}, f32[576,256]{1,0:T(8,128)S(1)}, u32[]{:S(2)}, u32[]{:S(2)}) collective-permute-start(f32[576,256]{1,0:T(8,128)} %copy.183), channel_id=1, source_target_pairs={{8,0},{16,8},{24,16},{9,1},{17,9},{25,17},{10,2},{18,10},{26,18},{... | collective-permute-start | bytes 1769480 | tf_op jit(solution)/shard_map/ppermute | solution.py:55
  85.7 17.7 %collective-permute-start.6 = (f32[576,256]{1,0:T(8,128)}, f32[576,256]{1,0:T(8,128)S(1)}, u32[]{:S(2)}, u32[]{:S(2)}) collective-permute-start(f32[576,256]{1,0:T(8,128)} %copy.182), channel_id=1, source_target_pairs={{0,8},{8,16},{16,24},{1,9},{9,17},{17,25},{2,10},{10,18},{18,26},{... | collective-permute-start | bytes 1769480 | tf_op jit(solution)/shard_map/ppermute | solution.py:54
  120.1 42.4 %all-to-all-start.3 = ((f32[8,2,4,48,256]{4,3,2,1,0:T(8,128)}), f32[8,2,4,48,256]{4,3,2,1,0:T(8,128)}, u32[]{:S(2)}, u32[]{:S(2)}) async-start(f32[8,2,4,48,256]{4,3,2,1,0:T(8,128)} %broadcast_select_fusion.4), calls=%async_computation.3 | async-start | bytes 6291456 | tf_op jit(solution)/shard_map/all_to_all | solution.py:39
  124.6 11.7 %collective-permute-start.8 = (f32[576,256]{1,0:T(8,128)S(1)}, f32[576,256]{1,0:T(8,128)}, u32[]{:S(2)}, u32[]{:S(2)}) collective-permute-start(f32[576,256]{1,0:T(8,128)S(1)} %collective-permute-done.6), channel_id=1, source_target_pairs={{8,16},{16,24},{9,17},{17,25},{10,18},{18,26},{11,19},{19,27},{12,... | collective-permute-start | bytes 1769480 | tf_op jit(solution)/shard_map/ppermute | solution.py:54
  126.1 17.6 %collective-permute-start.9 = (f32[576,256]{1,0:T(8,128)S(1)}, f32[576,256]{1,0:T(8,128)}, u32[]{:S(2)}, u32[]{:S(2)}) collective-permute-start(f32[576,256]{1,0:T(8,128)S(1)} %collective-permute-done.7), channel_id=1, source_target_pairs={{8,0},{16,8},{9,1},{17,9},{10,2},{18,10},{11,3},{19,11},{12,4},{20... | collective-permute-start | bytes 1769480 | tf_op jit(solution)/shard_map/ppermute | solution.py:55
  162.5 41.5 %all-to-all-start.4 = ((f32[8,2,4,48,256]{4,3,2,1,0:T(8,128)}), f32[8,2,4,48,256]{4,3,2,1,0:T(8,128)S(1)}, u32[]{:S(2)}, u32[]{:S(2)}) async-start(f32[8,2,4,48,256]{4,3,2,1,0:T(8,128)} %broadcast_select_fusion.3), calls=%async_computation.4 | async-start | bytes 6291456 | tf_op jit(solution)/shard_map/all_to_all | solution.py:39
  170.3 17.9 %collective-permute-start.11 = (f32[576,256]{1,0:T(8,128)}, f32[576,256]{1,0:T(8,128)}, u32[]{:S(2)}, u32[]{:S(2)}) collective-permute-start(f32[576,256]{1,0:T(8,128)} %collective-permute-done.9), channel_id=1, source_target_pairs={{8,0},{9,1},{10,2},{11,3},{12,4},{13,5},{14,6},{15,7}} | collective-permute-start | bytes 1769480 | tf_op jit(solution)/shard_map/ppermute | solution.py:55
  216.4 42.4 %all-to-all-start.9 = ((f32[8,2,4,48,256]{4,3,2,1,0:T(8,128)}), f32[8,2,4,48,256]{4,3,2,1,0:T(8,128)}, u32[]{:S(2)}, u32[]{:S(2)}) async-start(f32[8,2,4,48,256]{4,3,2,1,0:T(8,128)} %broadcast_select_fusion), calls=%async_computation.9 | async-start | bytes 6291456 | tf_op jit(solution)/shard_map/all_to_all | solution.py:39
  258.7 42.6 %all-to-all-start.7 = ((f32[8,2,4,48,256]{4,3,2,1,0:T(8,128)}), f32[8,2,4,48,256]{4,3,2,1,0:T(8,128)}, u32[]{:S(2)}, u32[]{:S(2)}) async-start(f32[8,2,4,48,256]{4,3,2,1,0:T(8,128)} %broadcast_select_fusion.1), calls=%async_computation.7 | async-start | bytes 6291456 | tf_op jit(solution)/shard_map/all_to_all | solution.py:39
  301.3 43.3 %all-to-all-start.5 = ((f32[8,2,4,48,256]{4,3,2,1,0:T(8,128)}), f32[8,2,4,48,256]{4,3,2,1,0:T(8,128)}, u32[]{:S(2)}, u32[]{:S(2)}) async-start(f32[8,2,4,48,256]{4,3,2,1,0:T(8,128)} %broadcast_select_fusion.2), calls=%async_computation.5 | async-start | bytes 6291456 | tf_op jit(solution)/shard_map/all_to_all | solution.py:39
  344.6 42.5 %all-to-all-start.10 = ((f32[8,2,4,48,256]{4,3,2,1,0:T(8,128)}), f32[8,2,4,48,256]{4,3,2,1,0:T(8,128)}, u32[]{:S(2)}, u32[]{:S(2)}) async-start(f32[8,2,4,48,256]{4,3,2,1,0:T(8,128)} %copy.212), calls=%async_computation.10 | async-start | bytes 6291456 | tf_op jit(solution)/shard_map/all_to_all | solution.py:39
  387.1 42.6 %all-to-all-start.6 = ((f32[8,2,4,48,256]{4,3,2,1,0:T(8,128)}), f32[8,2,4,48,256]{4,3,2,1,0:T(8,128)}, u32[]{:S(2)}, u32[]{:S(2)}) async-start(f32[8,2,4,48,256]{4,3,2,1,0:T(8,128)} %copy.196), calls=%async_computation.6 | async-start | bytes 6291456 | tf_op jit(solution)/shard_map/all_to_all | solution.py:39
  429.7 42.4 %all-to-all-start.8 = ((f32[8,2,4,48,256]{4,3,2,1,0:T(8,128)}), f32[8,2,4,48,256]{4,3,2,1,0:T(8,128)}, u32[]{:S(2)}, u32[]{:S(2)}) async-start(f32[8,2,4,48,256]{4,3,2,1,0:T(8,128)} %copy.204), calls=%async_computation.8 | async-start | bytes 6291456 | tf_op jit(solution)/shard_map/all_to_all | solution.py:39
  483.7 42.5 %all-to-all-start.11 = ((f32[8,2,4,48,256]{4,3,2,1,0:T(8,128)}), f32[8,2,4,48,256]{4,3,2,1,0:T(8,128)}, u32[]{:S(2)}, u32[]{:S(2)}) async-start(f32[8,2,4,48,256]{4,3,2,1,0:T(8,128)} %copy.219), calls=%async_computation.11 | async-start | bytes 6291456 | tf_op jit(solution)/shard_map/all_to_all | solution.py:39
  496.5 10.2 %collective-permute-start.13 = (f32[12,48,256]{2,1,0:T(8,128)S(1)}, f32[12,48,256]{2,1,0:T(8,128)}, u32[]{:S(2)}, u32[]{:S(2)}) collective-permute-start(f32[12,48,256]{2,1,0:T(8,128)S(1)} %copy.218), channel_id=1, source_target_pairs={{24,16},{25,17},{26,18},{27,19},{28,20},{29,21},{30,22},{31,23}} | collective-permute-start | bytes 1769480 | tf_op jit(solution)/shard_map/ppermute | solution.py:87
  498.0 14.6 %collective-permute-start.12 = (f32[12,48,256]{2,1,0:T(8,128)S(1)}, f32[12,48,256]{2,1,0:T(8,128)}, u32[]{:S(2)}, u32[]{:S(2)}) collective-permute-start(f32[12,48,256]{2,1,0:T(8,128)S(1)} %copy.217), channel_id=1, source_target_pairs={{0,8},{1,9},{2,10},{3,11},{4,12},{5,13},{6,14},{7,15}} | collective-permute-start | bytes 1769480 | tf_op jit(solution)/shard_map/ppermute | solution.py:86
  531.6 42.6 %all-to-all-start.12 = ((f32[8,2,4,48,256]{4,3,2,1,0:T(8,128)}), f32[8,2,4,48,256]{4,3,2,1,0:T(8,128)}, u32[]{:S(2)}, u32[]{:S(2)}) async-start(f32[8,2,4,48,256]{4,3,2,1,0:T(8,128)} %copy.224), calls=%async_computation.12 | async-start | bytes 6291456 | tf_op jit(solution)/shard_map/all_to_all | solution.py:39
  544.2 9.8 %collective-permute-start.15 = (f32[12,48,256]{2,1,0:T(8,128)S(1)}, f32[12,48,256]{2,1,0:T(8,128)}, u32[]{:S(2)}, u32[]{:S(2)}) collective-permute-start(f32[12,48,256]{2,1,0:T(8,128)S(1)} %copy.223), channel_id=1, source_target_pairs={{16,8},{24,16},{17,9},{25,17},{18,10},{26,18},{19,11},{27,19},{20,... | collective-permute-start | bytes 1769480 | tf_op jit(solution)/shard_map/ppermute | solution.py:87
  545.7 14.7 %collective-permute-start.14 = (f32[12,48,256]{2,1,0:T(8,128)S(1)}, f32[12,48,256]{2,1,0:T(8,128)}, u32[]{:S(2)}, u32[]{:S(2)}) collective-permute-start(f32[12,48,256]{2,1,0:T(8,128)S(1)} %copy.222), channel_id=1, source_target_pairs={{0,8},{8,16},{1,9},{9,17},{2,10},{10,18},{3,11},{11,19},{4,12},{12... | collective-permute-start | bytes 1769480 | tf_op jit(solution)/shard_map/ppermute | solution.py:86
  579.7 41.5 %all-to-all-start.13 = ((f32[8,2,4,48,256]{4,3,2,1,0:T(8,128)}), f32[8,2,4,48,256]{4,3,2,1,0:T(8,128)S(1)}, u32[]{:S(2)}, u32[]{:S(2)}) async-start(f32[8,2,4,48,256]{4,3,2,1,0:T(8,128)} %copy.229), calls=%async_computation.13 | async-start | bytes 6291456 | tf_op jit(solution)/shard_map/all_to_all | solution.py:39
  586.3 17.7 %collective-permute-start.17 = (f32[12,48,256]{2,1,0:T(8,128)S(1)}, f32[12,48,256]{2,1,0:T(8,128)S(1)}, u32[]{:S(2)}, u32[]{:S(2)}) collective-permute-start(f32[12,48,256]{2,1,0:T(8,128)S(1)} %copy.228), channel_id=1, source_target_pairs={{8,0},{16,8},{24,16},{9,1},{17,9},{25,17},{10,2},{18,10},{26,18},{... | collective-permute-start | bytes 1769480 | tf_op jit(solution)/shard_map/ppermute | solution.py:87
  587.6 17.4 %collective-permute-start.16 = (f32[12,48,256]{2,1,0:T(8,128)S(1)}, f32[12,48,256]{2,1,0:T(8,128)}, u32[]{:S(2)}, u32[]{:S(2)}) collective-permute-start(f32[12,48,256]{2,1,0:T(8,128)S(1)} %copy.227), channel_id=1, source_target_pairs={{0,8},{8,16},{16,24},{1,9},{9,17},{17,25},{2,10},{10,18},{18,26},{... | collective-permute-start | bytes 1769480 | tf_op jit(solution)/shard_map/ppermute | solution.py:86
  627.2 11.3 %collective-permute-start.25 = (f32[12,48,256]{2,1,0:T(8,128)S(1)}, f32[12,48,256]{2,1,0:T(8,128)S(1)}, u32[]{:S(2)}, u32[]{:S(2)}) collective-permute-start(f32[12,48,256]{2,1,0:T(8,128)S(1)} %copy.236), channel_id=1, source_target_pairs={{0,8},{1,9},{2,10},{3,11},{4,12},{5,13},{6,14},{7,15}} | collective-permute-start | bytes 1769480 | tf_op jit(solution)/shard_map/ppermute | solution.py:86
  629.0 14.2 %collective-permute-start.28 = (f32[12,48,256]{2,1,0:T(8,128)S(1)}, f32[12,48,256]{2,1,0:T(8,128)S(1)}, u32[]{:S(2)}, u32[]{:S(2)}) collective-permute-start(f32[12,48,256]{2,1,0:T(8,128)S(1)} %copy.239), channel_id=1, source_target_pairs={{24,16},{25,17},{26,18},{27,19},{28,20},{29,21},{30,22},{31,23}} | collective-permute-start | bytes 1769480 | tf_op jit(solution)/shard_map/ppermute | solution.py:87
  638.8 13.3 %collective-permute-start.26 = (f32[12,48,256]{2,1,0:T(8,128)S(1)}, f32[12,48,256]{2,1,0:T(8,128)S(1)}, u32[]{:S(2)}, u32[]{:S(2)}) collective-permute-start(f32[12,48,256]{2,1,0:T(8,128)S(1)} %fusion.24), channel_id=1, source_target_pairs={{0,8},{8,16},{1,9},{9,17},{2,10},{10,18},{3,11},{11,19},{4,12},{12... | collective-permute-start | bytes 1769480 | tf_op jit(solution)/shard_map/ppermute | solution.py:86
  643.7 14.9 %collective-permute-start.29 = (f32[12,48,256]{2,1,0:T(8,128)S(1)}, f32[12,48,256]{2,1,0:T(8,128)S(1)}, u32[]{:S(2)}, u32[]{:S(2)}) collective-permute-start(f32[12,48,256]{2,1,0:T(8,128)S(1)} %fusion.22), channel_id=1, source_target_pairs={{16,8},{24,16},{17,9},{25,17},{18,10},{26,18},{19,11},{27,19},{20,... | collective-permute-start | bytes 1769480 | tf_op jit(solution)/shard_map/ppermute | solution.py:87
  653.3 12.7 %collective-permute-start.27 = (f32[12,48,256]{2,1,0:T(8,128)}, f32[12,48,256]{2,1,0:T(8,128)}, u32[]{:S(2)}, u32[]{:S(2)}) collective-permute-start(f32[12,48,256]{2,1,0:T(8,128)} %fusion.23), channel_id=1, source_target_pairs={{0,8},{8,16},{16,24},{1,9},{9,17},{17,25},{2,10},{10,18},{18,26},{... | collective-permute-start | bytes 1769480 | tf_op jit(solution)/shard_map/ppermute | solution.py:86
  659.7 12.4 %collective-permute-start.30 = (f32[12,48,256]{2,1,0:T(8,128)}, f32[12,48,256]{2,1,0:T(8,128)}, u32[]{:S(2)}, u32[]{:S(2)}) collective-permute-start(f32[12,48,256]{2,1,0:T(8,128)} %fusion.21), channel_id=1, source_target_pairs={{8,0},{16,8},{24,16},{9,1},{17,9},{25,17},{10,2},{18,10},{26,18},{... | collective-permute-start | bytes 1769480 | tf_op jit(solution)/shard_map/ppermute | solution.py:87
  701.8 31.9 %collective-permute-start.24 = (f32[576,32]{0,1:T(8,128)}, f32[576,32]{0,1:T(8,128)}, u32[]{:S(2)}, u32[]{:S(2)}) collective-permute-start(f32[576,32]{0,1:T(8,128)} %bitcast.145), channel_id=1, source_target_pairs={{0,7},{1,6},{2,5},{3,4},{4,3},{5,2},{6,1},{7,0},{8,15},{9,14},{10,... | collective-permute-start | bytes 221192 | tf_op jit(solution)/shard_map/ppermute | solution.py:29
  707.3 25.0 %collective-permute-start.23 = (f32[576,32]{0,1:T(8,128)}, f32[576,32]{0,1:T(8,128)}, u32[]{:S(2)}, u32[]{:S(2)}) collective-permute-start(f32[576,32]{0,1:T(8,128)} %bitcast.143), channel_id=1, source_target_pairs={{0,6},{1,7},{2,4},{3,5},{4,2},{5,3},{6,0},{7,1},{8,14},{9,15},{10,... | collective-permute-start | bytes 221192 | tf_op jit(solution)/shard_map/ppermute | solution.py:29
  710.9 20.3 %collective-permute-start.22 = (f32[576,32]{0,1:T(8,128)}, f32[576,32]{0,1:T(8,128)}, u32[]{:S(2)}, u32[]{:S(2)}) collective-permute-start(f32[576,32]{0,1:T(8,128)} %bitcast.141), channel_id=1, source_target_pairs={{0,5},{1,4},{2,7},{3,6},{4,1},{5,0},{6,3},{7,2},{8,13},{9,12},{10,... | collective-permute-start | bytes 221192 | tf_op jit(solution)/shard_map/ppermute | solution.py:29
  713.0 15.5 %collective-permute-start.21 = (f32[576,32]{0,1:T(8,128)}, f32[576,32]{0,1:T(8,128)}, u32[]{:S(2)}, u32[]{:S(2)}) collective-permute-start(f32[576,32]{0,1:T(8,128)} %bitcast.139), channel_id=1, source_target_pairs={{0,4},{1,5},{2,6},{3,7},{4,0},{5,1},{6,2},{7,3},{8,12},{9,13},{10,... | collective-permute-start | bytes 221192 | tf_op jit(solution)/shard_map/ppermute | solution.py:29
  717.9 6.0 collective-permute-start.19
  728.3 7.5 %collective-permute-start.31 = (f32[576,32]{0,1:T(8,128)S(1)}, f32[576,32]{0,1:T(8,128)S(1)}, u32[]{:S(2)}, u32[]{:S(2)}) collective-permute-start(f32[576,32]{0,1:T(8,128)S(1)} %bitcast.422), channel_id=1, source_target_pairs={{0,1},{1,0},{2,3},{3,2},{4,5},{5,4},{6,7},{7,6},{8,9},{9,8},{10,11... | collective-permute-start | bytes 221192 | tf_op jit(solution)/shard_map/ppermute | solution.py:29
  728.4 9.1 %collective-permute-start.32 = (f32[576,32]{0,1:T(8,128)S(1)}, f32[576,32]{0,1:T(8,128)S(1)}, u32[]{:S(2)}, u32[]{:S(2)}) collective-permute-start(f32[576,32]{0,1:T(8,128)S(1)} %bitcast.421), channel_id=1, source_target_pairs={{0,2},{1,3},{2,0},{3,1},{4,6},{5,7},{6,4},{7,5},{8,10},{9,11},{10,... | collective-permute-start | bytes 221192 | tf_op jit(solution)/shard_map/ppermute | solution.py:29
  731.2 7.6 %collective-permute-start.33 = (f32[576,32]{0,1:T(8,128)S(1)}, f32[576,32]{0,1:T(8,128)S(1)}, u32[]{:S(2)}, u32[]{:S(2)}) collective-permute-start(f32[576,32]{0,1:T(8,128)S(1)} %bitcast.420), channel_id=1, source_target_pairs={{0,3},{1,2},{2,1},{3,0},{4,7},{5,6},{6,5},{7,4},{8,11},{9,10},{10,... | collective-permute-start | bytes 221192 | tf_op jit(solution)/shard_map/ppermute | solution.py:29
  732.3 6.5 collective-permute-start.34
  733.7 5.2 collective-permute-start.35
  735.8 5.9 collective-permute-start.36
  737.5 5.9 collective-permute-start.37
  (69 other events, 677.6 us)
